TPU v7x, 128 devices: a whole 4x4x4 slice. The times are simulated.
128 devices in a mesh: ctx: 32 (over y, z, core), tp: 4 (over x).
Axes of the slice: x: 4, y: 4, z: 4, core: 2. Of those that a mesh axis runs over, the one named last changes fastest.
Arguments:
- hidden_in: bfloat16 [16384, 4608], P('ctx'), may hold values from -5.4 to 5.4
- pre_gain: float32 [4608], replicated, may hold values from 0.25 to 1.75
- w_query: bfloat16 [4608, 2048], P(None, 'tp'), may hold values from -0.677644 to 0.677644
- w_key: bfloat16 [4608, 1024], P(None, 'tp'), may hold values from -0.058925565 to 0.058925565
- w_value: bfloat16 [4608, 1024], P(None, 'tp'), may hold values from -0.09375 to 0.09375
- w_out: bfloat16 [2048, 4608], P('tp'), may hold values from -0.26516504 to 0.26516504
- post_gain: float32 [4608], P('tp'), may hold values from 0.25 to 1.75
Outputs:
- layer_out: bfloat16 [16384, 4608], P('ctx', 'tp')
- sink_share: float32 [16384], P('ctx')
All inputs are finite; a program needn't handle non-finite values.
Results may differ from a plain program's by a relative error of at most 0.0095.
The roundings to bfloat16 on the way count: a program that leaves them out, or rounds other values in their place, can miss the bound.
Values may be sent and summed in bfloat16 or wider, within the bound.
No kernel may reach another device: no remote copies, remote signals or barrier semaphores. Data moves between devices by JAX's collectives and lax.ppermute only.
A program may use at most 192 MiB of HBM per device.

v0:
```python
import jax
import jax.numpy as jnp
from jax import lax
from jax.sharding import PartitionSpec as P

D = 4608
QHEADS = 16
HEAD = 128
WINDOW = 4096
SINKS = 4


def shifted(x, axis, by):
    devices = lax.axis_size(axis)
    pairs = [(i, i + by) for i in range(devices) if 0 <= i + by < devices]
    return lax.ppermute(x, axis, pairs)


def spread(value, axis, source):
    kept = jnp.where(lax.axis_index(axis) == source, value, 0).astype(value.dtype)
    return lax.psum(kept, axis)


def rope_tables(positions):
    index = jnp.arange(0, HEAD, 2).astype(jnp.float32)
    inverse = jnp.exp(-jnp.log(jnp.float32(10000.0)) * index / HEAD)
    angles = positions.astype(jnp.float32)[:, None] * inverse[None, :]
    angles = jnp.concatenate([angles, angles], axis=1)
    return (jnp.cos(angles)[:, None, :], jnp.sin(angles)[:, None, :])


def rotate(values, cosine_table, sine_table):
    half = values.shape[-1] // 2
    turned = jnp.concatenate([-values[..., half:], values[..., :half]], axis=-1)
    return values * cosine_table + turned * sine_table


def project_keys(states, w_key, w_value, positions):
    count = states.shape[0]
    cosine_table, sine_table = rope_tables(positions)
    keys = jnp.dot(states, w_key, preferred_element_type=jnp.float32).reshape(count, -1, HEAD)
    keys = rotate(keys, cosine_table, sine_table).astype(jnp.bfloat16).reshape(count, -1)
    values = jnp.dot(states, w_value, preferred_element_type=jnp.float32).astype(jnp.bfloat16)
    return (keys, values)


def on_device(hidden_in, pre_gain, w_query, w_key, w_value, w_out, post_gain):
    tok_rows = hidden_in.shape[0]
    local_q = w_query.shape[1] // HEAD
    local_kv = w_key.shape[1] // HEAD
    group = local_q // local_kv
    offset = lax.axis_index("ctx") * tok_rows
    inputs = hidden_in.astype(jnp.float32)
    normed = (
        inputs * lax.rsqrt(jnp.mean(inputs * inputs, axis=-1, keepdims=True) + 1e-06) * pre_gain
    ).astype(jnp.bfloat16)
    positions = offset + jnp.arange(tok_rows, dtype=jnp.int32)
    cosine_table, sine_table = rope_tables(positions)
    query = jnp.dot(normed, w_query, preferred_element_type=jnp.float32).reshape(
        tok_rows, local_q, HEAD
    )
    query = (
        rotate(query, cosine_table, sine_table)
        .astype(jnp.bfloat16)
        .reshape(tok_rows, local_kv, group, HEAD)
    )
    keys, values = project_keys(normed, w_key, w_value, positions)
    reach = WINDOW // tok_rows
    pieces = []
    for distance in range(reach, 0, -1):
        pieces.append(shifted((keys, values), "ctx", distance))
    keys_all = jnp.concatenate([piece[0] for piece in pieces] + [keys], axis=0)
    values_all = jnp.concatenate([piece[1] for piece in pieces] + [values], axis=0)
    sink_keys, sink_values = (spread(keys[:SINKS], "ctx", 0), spread(values[:SINKS], "ctx", 0))
    sink_keys = sink_keys.reshape(SINKS, local_kv, HEAD)
    sink_values = sink_values.reshape(SINKS, local_kv, HEAD)
    block_rows = min(512, tok_rows)
    span = WINDOW + block_rows

    def one_block(block_index):
        start = block_index * block_rows
        key_block = keys_all.reshape(span, local_kv, HEAD)
        value_block = values_all.reshape(span, local_kv, HEAD)
        scores = (
            jnp.einsum("qkgd,lkd->kgql", query, key_block, preferred_element_type=jnp.float32)
            / 12.0
        )
        scores = 50.0 * jnp.tanh(scores / 50.0)
        sink_scores = (
            jnp.einsum("qkgd,lkd->kgql", query, sink_keys, preferred_element_type=jnp.float32)
            / 12.0
        )
        sink_scores = 50.0 * jnp.tanh(sink_scores / 50.0)
        query_pos = offset + start + jnp.arange(block_rows, dtype=jnp.int32)
        key_pos = offset + start - WINDOW + jnp.arange(span, dtype=jnp.int32)
        distance_map = query_pos[:, None] - key_pos[None, :]
        live = (key_pos[None, :] >= SINKS) & (distance_map >= 0) & (distance_map < WINDOW)
        sink_live = query_pos[:, None] - jnp.arange(SINKS, dtype=jnp.int32)[None, :] >= 0
        expo = jnp.where(live, jnp.exp(scores), 0.0)
        sink_expo = jnp.where(sink_live, jnp.exp(sink_scores), 0.0)
        total = jnp.sum(expo, axis=-1) + jnp.sum(sink_expo, axis=-1)
        weight = expo / total[..., None]
        sink_weight = sink_expo / total[..., None]
        sink_sum = jnp.sum(sink_expo, axis=-1)
        attended = jnp.einsum(
            "kgql,lkd->qkgd",
            weight.astype(jnp.bfloat16),
            value_block,
            preferred_element_type=jnp.float32,
        )
        attended = attended + jnp.einsum(
            "kgql,lkd->qkgd",
            sink_weight.astype(jnp.bfloat16),
            sink_values,
            preferred_element_type=jnp.float32,
        )
        attended = attended.astype(jnp.bfloat16).reshape(block_rows, local_q * HEAD)
        return (attended, jnp.sum(sink_sum, axis=(0, 1)))

    attended, sink_sums = lax.map(one_block, jnp.arange(tok_rows // block_rows, dtype=jnp.int32))
    attended = attended.reshape(tok_rows, local_q * HEAD)
    sink_sums = sink_sums.reshape(tok_rows)
    cols_dev = post_gain.shape[0]
    partial_rows = jnp.dot(attended, w_out, preferred_element_type=jnp.float32)
    projected = lax.psum_scatter(partial_rows, "tp", scatter_dimension=1, tiled=True)
    squares = jnp.sum(projected * projected, axis=-1)
    total_squares, total_sinks = lax.psum((squares, sink_sums), "tp")
    post = projected * lax.rsqrt(total_squares / D + 1e-06)[:, None] * post_gain
    own_cols = lax.dynamic_slice_in_dim(inputs, lax.axis_index("tp") * cols_dev, cols_dev, 1)
    layer_out = (own_cols + post).astype(jnp.bfloat16)
    sink_share = jnp.log(total_sinks / QHEADS)
    return (layer_out, sink_share)


def solution(mesh):
    return jax.shard_map(
        on_device,
        mesh=mesh,
        in_specs=(
            P("ctx", None),
            P(),
            P(None, "tp"),
            P(None, "tp"),
            P(None, "tp"),
            P("tp", None),
            P("tp"),
        ),
        out_specs=(P("ctx", "tp"), P("ctx")),
        check_vma=False,
    )
```

profile of v0, /device:TPU:0, one launch (start us, length us, event | category | flops | bytes accessed | tf_op | source)
XLA Modules:
  0.0 350.9 jit_solution(993814466093420945)
XLA Ops:
  8.6 3.6 %multiply_reduce_fusion = f32[512]{0:T(512)S(1)} fusion(bf16[512,4608]{1,0:T(8,128)(2,1)} %param.7), kind=kLoop, calls=%fused_computation.7 | loop fusion | flops 7077376 | bytes 4720640 | tf_op jit(solution)/shard_map/reduce_sum | solution.py:55
  16.2 4.4 %collective-permute-start.8 = (bf16[512,256]{0,1:T(8,128)(2,1)}, bf16[512,256]{0,1:T(8,128)(2,1)}, u32[]{:S(2)}, u32[]{:S(2)}) collective-permute-start(bf16[512,256]{0,1:T(8,128)(2,1)} %fusion.15), channel_id=1, source_target_pairs={{0,32},{4,36},{8,40},{12,44},{16,48},{20,52},{24,56},{28,60},{32,6... | collective-permute-start | bytes 786440 | tf_op jit(solution)/shard_map/ppermute | solution.py:16
  20.7 5.8 %collective-permute-start.9 = (bf16[512,256]{0,1:T(8,128)(2,1)}, bf16[512,256]{0,1:T(8,128)(2,1)}, u32[]{:S(2)}, u32[]{:S(2)}) collective-permute-start(bf16[512,256]{0,1:T(8,128)(2,1)} %fusion.15), channel_id=1, source_target_pairs={{0,28},{4,32},{8,36},{12,40},{16,44},{20,48},{24,52},{28,56},{32,6... | collective-permute-start | bytes 786440 | tf_op jit(solution)/shard_map/ppermute | solution.py:16
  26.5 3.3 collective-permute-start.10
  29.8 3.0 collective-permute-start.11
  32.8 5.2 %convolution_convert_fusion = bf16[512,256]{1,0:T(8,128)(2,1)} fusion(bf16[4608,256]{1,0:T(8,128)(2,1)} %param.11, f32[4608]{0:T(1024)S(1)} %copy-done.14, f32[512]{0:T(512)S(1)} %add_rsqrt_fusion.1, bf16[512,4608]{1,0:T(8,128)(2,1)} %param.7), kind=kOutput, calls=%fused_computation.16 | convolution fusion | flops 1217527808 | bytes 7360512 | tf_op jit(solution)/shard_map/dot_general | solution.py:43
  38.1 2.0 collective-permute-start
  40.7 6.9 %fusion.29 = f32[512,512]{0,1:T(8,128)S(1)} fusion(bf16[4608,512]{1,0:T(8,128)(2,1)} %param.9, f32[4608]{0:T(1024)S(1)} %copy-done.15, f32[512]{0:T(512)} %copy-done.13, bf16[512,4608]{1,0:T(8,128)(2,1)} %param.7), kind=kOutput, calls=%fused_computation.75 | convolution fusion | flops 2425356288 | bytes 10506240 | tf_op jit(solution)/shard_map/dot_general | solution.py:59
  53.3 4.7 %fusion.3 = pred[512,4608]{0,1:T(8,128)(4,1)} fusion(s32[4608]{0:T(1024)S(1)} %copy-done.11, s32[512]{0:T(512)S(1)} %iota_add_fusion.1, pred[4608]{0:T(1024)(128)(4,1)S(1)} %broadcast_compare_fusion), kind=kLoop, calls=%fused_computation.9 | loop fusion | flops 11796480 | bytes 2384384 | tf_op jit(solution)/shard_map/while/body/eval_jaxpr/and | solution.py:97
  59.4 62.8 %all-reduce.1 = (bf16[4,2,128]{2,0,1:T(4,128)(2,1)S(1)}, bf16[4,2,128]{2,0,1:T(4,128)(2,1)S(1)}) all-reduce(bf16[4,2,128]{2,0,1:T(4,128)(2,1)S(1)} %fusion.21, bf16[4,2,128]{2,0,1:T(4,128)(2,1)S(1)} %fusion.22), channel_id=1, replica_groups=mesh['ctx'=32,'tp'=4] {'ctx'}, use_global_device_ids=true, to_apply=%region_2.3 | all-reduce | flops 2048 | bytes 8192 | tf_op jit(solution)/shard_map/psum | solution.py:21
  133.1 7.4 %collective-permute-done.1 = bf16[512,256]{1,0:T(8,128)(2,1)S(1)} collective-permute-done((bf16[512,256]{1,0:T(8,128)(2,1)}, bf16[512,256]{1,0:T(8,128)(2,1)S(1)}, u32[]{:S(2)}, u32[]{:S(2)}) %collective-permute-start.1) | collective-permute-done | bytes 262176 | tf_op jit(solution)/shard_map/ppermute | solution.py:16
  141.9 7.1 %collective-permute-start.14 = (bf16[512,256]{0,1:T(8,128)(2,1)}, bf16[512,256]{0,1:T(8,128)(2,1)}, u32[]{:S(2)}, u32[]{:S(2)}) collective-permute-start(bf16[512,256]{0,1:T(8,128)(2,1)} %fusion.15), channel_id=1, source_target_pairs={{0,8},{4,12},{8,16},{12,20},{16,24},{20,28},{24,32},{28,36},{32,40... | collective-permute-start | bytes 786440 | tf_op jit(solution)/shard_map/ppermute | solution.py:16
  149.0 2.4 collective-permute-start.15
  151.4 2.0 collective-permute-start.5
  153.5 4.7 %collective-permute-start.6 = (bf16[512,256]{1,0:T(8,128)(2,1)}, bf16[512,256]{1,0:T(8,128)(2,1)}, u32[]{:S(2)}, u32[]{:S(2)}) collective-permute-start(bf16[512,256]{1,0:T(8,128)(2,1)} %convolution_convert_fusion), channel_id=1, source_target_pairs={{0,8},{4,12},{8,16},{12,20},{16,24},{20,28},{24,32},{28,36},{32,40... | collective-permute-start | bytes 786440 | tf_op jit(solution)/shard_map/ppermute | solution.py:16
  158.2 2.0 collective-permute-start.7
  173.8 2.5 copy.34
  186.1 17.2 %fusion = (f32[2,2,512]{2,1,0:T(2,128)S(1)}, f32[2,4608,512,2]{2,1,3,0:T(8,128)}) fusion(pred[512,4608]{0,1:T(8,128)(4,1)S(1)} %copy-done.6, bf16[512,2,2,128]{3,0,2,1:T(8,128)(2,1)S(1)} %copy-done.9, bf16[4608,2,128]{2,0,1:T(8,128)(2,1)} %constant_dynamic-update-slice_fusion.9), kind=kOutput, calls=%fused_computation.2 | convolution fusion | flops 2453665792 | bytes 42999808 | tf_op jit(solution)/shard_map/while/body/eval_jaxpr/qkgd,lkd->kgql/dot_general | solution.py:85
  203.6 19.5 %fusion.7 = bf16[2,128,2,512]{3,1,2,0:T(8,128)(2,1)} fusion(f32[2,128,2,512]{3,1,2,0:T(8,128)S(1)} %fusion.18, bf16[4608,2,128,1]{0,2,3,1:T(8,128)(2,1)} %bitcast.80, f32[2,4608,512,2]{2,1,3,0:T(8,128)} %get-tuple-element.42, f32[2,2,512]{2,1,0:T(2,128)S(1)} %add.103, pred[512,4608]{0,1:T(8,128)(4,1)S(1)} %copy-done.6), kind=kOutput, calls=%fused_computation.15 | convolution fusion | flops 2463629312 | bytes 44048384 | tf_op jit(solution)/shard_map/while/body/eval_jaxpr/kgql,lkd->qkgd/dot_general | solution.py:105
  223.1 8.8 %fusion.33 = f32[512,4608]{1,0:T(8,128)} fusion(bf16[512,512]{0,1:T(8,128)(2,1)} %bitcast.81, bf16[512,4608]{1,0:T(8,128)(2,1)} %param.12), kind=kOutput, calls=%fused_computation.79 | convolution fusion | flops 2415919104 | bytes 14680064 | tf_op jit(solution)/shard_map/dot_general | solution.py:124
  231.9 7.2 %convert_element_type.56 = f32[512,4608]{1,0:T(8,128)} convert(bf16[512,4608]{1,0:T(8,128)(2,1)} %param.7) | non-fusion elementwise | flops 2359296 | bytes 14155776 | tf_op jit(solution)/shard_map/convert_element_type | solution.py:53
  239.1 89.9 %reduce-scatter.2.cloned.1.call-done = f32[512,1152]{1,0:T(8,128)} async-done(((f32[512,4608]{1,0:T(8,128)}), f32[512,1152]{1,0:T(8,128)}) %reduce-scatter.2.cloned.1.call-update) | async-done | bytes 2359312 | tf_op jit(solution)/shard_map/reduce_scatter | solution.py:125
  331.0 8.6 %all-reduce = (f32[512]{0:T(512)S(1)}, f32[512]{0:T(512)S(1)}) all-reduce(f32[512]{0:T(512)S(1)} %multiply_reduce_fusion.1, f32[512]{0:T(512)S(1)} %get-tuple-element.20), channel_id=1, replica_groups=mesh['ctx'=32,'tp'=4] {'tp'}, use_global_device_ids=true, to_apply=%region_7.8 | all-reduce | flops 1024 | bytes 8192 | tf_op jit(solution)/shard_map/psum | solution.py:127
  340.1 3.9 %add_convert_fusion = bf16[512,1152]{1,0:T(8,128)(2,1)} fusion(f32[512,1152]{1,0:T(8,128)} %reduce-scatter.2.cloned.1.call-done, f32[512,4608]{1,0:T(8,128)} %convert_element_type.56, s32[]{:T(128)S(6)} %select_n.30, f32[1152]{0:T(1024)S(1)} %copy-done.12, f32[512]{0:T(512)S(1)} %get-tuple-element.45), kind=kLoop, calls=%fused_computation.12 | loop fusion | flops 2359296 | bytes 5904900 | tf_op jit(solution)/shard_map/convert_element_type | solution.py:130
  (115 shorter events, 51.3 us)
Async XLA Ops:
  7.2 321.9 %reduce-scatter.2.cloned.1.call-start = ((), (), s32[]{:S(2)}) async-start(), calls=%async_computation.1 | async-start | bytes 11796480 | tf_op jit(solution)/shard_map/reduce_scatter | solution.py:125
  8.5 32.1 %copy-start.3 = (f32[512,128]{1,0:T(8,128)}, f32[512,128]{1,0:T(8,128)S(1)}, u32[]{:S(2)}) copy-start(f32[512,128]{1,0:T(8,128)S(1)} %get-tuple-element.39) | copy-start | bytes 786436
  12.6 20.3 %copy-start.13 = (f32[512]{0:T(512)}, f32[512]{0:T(512)S(1)}, u32[]{:S(2)}) copy-start(f32[512]{0:T(512)S(1)} %add_rsqrt_fusion.1) | copy-start | bytes 6148
  15.1 23.0 %copy-start.7 = (f32[512,2,128]{2,0,1:T(8,128)}, f32[512,2,128]{2,0,1:T(8,128)S(1)}, u32[]{:S(2)}) copy-start(f32[512,2,128]{2,0,1:T(8,128)S(1)} %maximum_multiply_fusion.1) | copy-start | bytes 1572868
  16.2 24.5 %copy-start.15 = (f32[4608]{0:T(1024)S(1)}, f32[4608]{0:T(1024)}, u32[]{:S(2)}) copy-start(f32[4608]{0:T(1024)} %param.8) | copy-start | bytes 55300
  16.2 106.0 %collective-permute-start.8 = (bf16[512,256]{0,1:T(8,128)(2,1)}, bf16[512,256]{0,1:T(8,128)(2,1)}, u32[]{:S(2)}, u32[]{:S(2)}) collective-permute-start(bf16[512,256]{0,1:T(8,128)(2,1)} %fusion.15), channel_id=1, source_target_pairs={{0,32},{4,36},{8,40},{12,44},{16,48},{20,52},{24,56},{28,60},{32,6... | collective-permute-start | bytes 786440 | tf_op jit(solution)/shard_map/ppermute | solution.py:16
  20.7 105.4 %collective-permute-start.9 = (bf16[512,256]{0,1:T(8,128)(2,1)}, bf16[512,256]{0,1:T(8,128)(2,1)}, u32[]{:S(2)}, u32[]{:S(2)}) collective-permute-start(bf16[512,256]{0,1:T(8,128)(2,1)} %fusion.15), channel_id=1, source_target_pairs={{0,28},{4,32},{8,36},{12,40},{16,44},{20,48},{24,52},{28,56},{32,6... | collective-permute-start | bytes 786440 | tf_op jit(solution)/shard_map/ppermute | solution.py:16
  26.5 101.0 %collective-permute-start.10 = (bf16[512,256]{0,1:T(8,128)(2,1)}, bf16[512,256]{0,1:T(8,128)(2,1)}, u32[]{:S(2)}, u32[]{:S(2)}) collective-permute-start(bf16[512,256]{0,1:T(8,128)(2,1)} %fusion.15), channel_id=1, source_target_pairs={{0,24},{4,28},{8,32},{12,36},{16,40},{20,44},{24,48},{28,52},{32,5... | collective-permute-start | bytes 786440 | tf_op jit(solution)/shard_map/ppermute | solution.py:16
  29.8 99.0 %collective-permute-start.11 = (bf16[512,256]{0,1:T(8,128)(2,1)}, bf16[512,256]{0,1:T(8,128)(2,1)}, u32[]{:S(2)}, u32[]{:S(2)}) collective-permute-start(bf16[512,256]{0,1:T(8,128)(2,1)} %fusion.15), channel_id=1, source_target_pairs={{0,20},{4,24},{8,28},{12,32},{16,36},{20,40},{24,44},{28,48},{32,5... | collective-permute-start | bytes 786440 | tf_op jit(solution)/shard_map/ppermute | solution.py:16
  38.1 92.7 %collective-permute-start = (bf16[512,256]{1,0:T(8,128)(2,1)}, bf16[512,256]{1,0:T(8,128)(2,1)}, u32[]{:S(2)}, u32[]{:S(2)}) collective-permute-start(bf16[512,256]{1,0:T(8,128)(2,1)} %convolution_convert_fusion), channel_id=1, source_target_pairs={{0,32},{4,36},{8,40},{12,44},{16,48},{20,52},{24,56},{28,60},{32,6... | collective-permute-start | bytes 786440 | tf_op jit(solution)/shard_map/ppermute | solution.py:16
  53.3 77.5 %copy-start.8 = (bf16[512,2,2,128]{3,0,2,1:T(8,128)(2,1)}, bf16[512,2,2,128]{3,0,2,1:T(8,128)(2,1)S(1)}, u32[]{:S(2)}) copy-start(bf16[512,2,2,128]{3,0,2,1:T(8,128)(2,1)S(1)} %fusion.14) | copy-start | bytes 1572868
  122.3 18.2 %collective-permute-start.1 = (bf16[512,256]{1,0:T(8,128)(2,1)}, bf16[512,256]{1,0:T(8,128)(2,1)S(1)}, u32[]{:S(2)}, u32[]{:S(2)}) collective-permute-start(bf16[512,256]{1,0:T(8,128)(2,1)} %convolution_convert_fusion), channel_id=1, source_target_pairs={{0,28},{4,32},{8,36},{12,40},{16,44},{20,48},{24,52},{28,56},{32,6... | collective-permute-start | bytes 786440 | tf_op jit(solution)/shard_map/ppermute | solution.py:16
  126.1 15.7 %collective-permute-start.12 = (bf16[512,256]{0,1:T(8,128)(2,1)}, bf16[512,256]{0,1:T(8,128)(2,1)S(1)}, u32[]{:S(2)}, u32[]{:S(2)}) collective-permute-start(bf16[512,256]{0,1:T(8,128)(2,1)} %fusion.15), channel_id=1, source_target_pairs={{0,16},{4,20},{8,24},{12,28},{16,32},{20,36},{24,40},{28,44},{32,4... | collective-permute-start | bytes 786440 | tf_op jit(solution)/shard_map/ppermute | solution.py:16
  127.5 21.5 %collective-permute-start.13 = (bf16[512,256]{0,1:T(8,128)(2,1)}, bf16[512,256]{0,1:T(8,128)(2,1)S(1)}, u32[]{:S(2)}, u32[]{:S(2)}) collective-permute-start(bf16[512,256]{0,1:T(8,128)(2,1)} %fusion.15), channel_id=1, source_target_pairs={{0,12},{4,16},{8,20},{12,24},{16,28},{20,32},{24,36},{28,40},{32,4... | collective-permute-start | bytes 786440 | tf_op jit(solution)/shard_map/ppermute | solution.py:16
  128.8 22.7 %collective-permute-start.2 = (bf16[512,256]{1,0:T(8,128)(2,1)}, bf16[512,256]{1,0:T(8,128)(2,1)S(1)}, u32[]{:S(2)}, u32[]{:S(2)}) collective-permute-start(bf16[512,256]{1,0:T(8,128)(2,1)} %convolution_convert_fusion), channel_id=1, source_target_pairs={{0,24},{4,28},{8,32},{12,36},{16,40},{20,44},{24,48},{28,52},{32,5... | collective-permute-start | bytes 786440 | tf_op jit(solution)/shard_map/ppermute | solution.py:16
  130.8 22.6 %collective-permute-start.3 = (bf16[512,256]{1,0:T(8,128)(2,1)}, bf16[512,256]{1,0:T(8,128)(2,1)S(1)}, u32[]{:S(2)}, u32[]{:S(2)}) collective-permute-start(bf16[512,256]{1,0:T(8,128)(2,1)} %convolution_convert_fusion), channel_id=1, source_target_pairs={{0,20},{4,24},{8,28},{12,32},{16,36},{20,40},{24,44},{28,48},{32,5... | collective-permute-start | bytes 786440 | tf_op jit(solution)/shard_map/ppermute | solution.py:16
  140.5 17.6 %collective-permute-start.4 = (bf16[512,256]{1,0:T(8,128)(2,1)}, bf16[512,256]{1,0:T(8,128)(2,1)S(1)}, u32[]{:S(2)}, u32[]{:S(2)}) collective-permute-start(bf16[512,256]{1,0:T(8,128)(2,1)} %convolution_convert_fusion), channel_id=1, source_target_pairs={{0,16},{4,20},{8,24},{12,28},{16,32},{20,36},{24,40},{28,44},{32,4... | collective-permute-start | bytes 786440 | tf_op jit(solution)/shard_map/ppermute | solution.py:16
  141.9 24.4 %collective-permute-start.14 = (bf16[512,256]{0,1:T(8,128)(2,1)}, bf16[512,256]{0,1:T(8,128)(2,1)}, u32[]{:S(2)}, u32[]{:S(2)}) collective-permute-start(bf16[512,256]{0,1:T(8,128)(2,1)} %fusion.15), channel_id=1, source_target_pairs={{0,8},{4,12},{8,16},{12,20},{16,24},{20,28},{24,32},{28,36},{32,40... | collective-permute-start | bytes 786440 | tf_op jit(solution)/shard_map/ppermute | solution.py:16
  149.0 11.2 %copy-start.10 = (bf16[512,256]{0,1:T(8,128)(2,1)}, bf16[512,256]{0,1:T(8,128)(2,1)S(1)}, u32[]{:S(2)}) copy-start(bf16[512,256]{0,1:T(8,128)(2,1)S(1)} %collective-permute-done.13) | copy-start | bytes 786436
  149.0 19.0 %collective-permute-start.15 = (bf16[512,256]{0,1:T(8,128)(2,1)}, bf16[512,256]{0,1:T(8,128)(2,1)}, u32[]{:S(2)}, u32[]{:S(2)}) collective-permute-start(bf16[512,256]{0,1:T(8,128)(2,1)} %fusion.15), channel_id=1, source_target_pairs={{0,4},{4,8},{8,12},{12,16},{16,20},{20,24},{24,28},{28,32},{32,36}... | collective-permute-start | bytes 786440 | tf_op jit(solution)/shard_map/ppermute | solution.py:16
  151.4 18.4 %collective-permute-start.5 = (bf16[512,256]{1,0:T(8,128)(2,1)}, bf16[512,256]{1,0:T(8,128)(2,1)}, u32[]{:S(2)}, u32[]{:S(2)}) collective-permute-start(bf16[512,256]{1,0:T(8,128)(2,1)} %convolution_convert_fusion), channel_id=1, source_target_pairs={{0,12},{4,16},{8,20},{12,24},{16,28},{20,32},{24,36},{28,40},{32,4... | collective-permute-start | bytes 786440 | tf_op jit(solution)/shard_map/ppermute | solution.py:16
  153.5 17.3 %collective-permute-start.6 = (bf16[512,256]{1,0:T(8,128)(2,1)}, bf16[512,256]{1,0:T(8,128)(2,1)}, u32[]{:S(2)}, u32[]{:S(2)}) collective-permute-start(bf16[512,256]{1,0:T(8,128)(2,1)} %convolution_convert_fusion), channel_id=1, source_target_pairs={{0,8},{4,12},{8,16},{12,20},{16,24},{20,28},{24,32},{28,36},{32,40... | collective-permute-start | bytes 786440 | tf_op jit(solution)/shard_map/ppermute | solution.py:16
  158.2 13.6 %collective-permute-start.7 = (bf16[512,256]{1,0:T(8,128)(2,1)}, bf16[512,256]{1,0:T(8,128)(2,1)}, u32[]{:S(2)}, u32[]{:S(2)}) collective-permute-start(bf16[512,256]{1,0:T(8,128)(2,1)} %convolution_convert_fusion), channel_id=1, source_target_pairs={{0,4},{4,8},{8,12},{12,16},{16,20},{20,24},{24,28},{28,32},{32,36}... | collective-permute-start | bytes 786440 | tf_op jit(solution)/shard_map/ppermute | solution.py:16
  239.1 101.0 %copy-start.12 = (f32[1152]{0:T(1024)S(1)}, f32[1152]{0:T(1024)}, u32[]{:S(2)}) copy-start(f32[1152]{0:T(1024)} %param.13) | copy-start | bytes 13828
  (9 other events, 48.4 us)
Sparse Core Ops, SparseCore 0:
  232.0 97.0 reduce-scatter.1
where the time goes:
time: 352 us; the launch traced here: 351 us
  waiting for transfers between devices  97.4 us (28%)
  blocking collectives  71.4 us (20%)
  matrix products  60 us (17%)
  starting transfers between devices  44.7 us (13%)
  local copies, waits for them, and re-layouts  34.1 us (10%)
  other arithmetic  28.8 us (8%)
  between operations  14.5 us (4%)
    reduce_scatter x1, waiting for transfers between devices, on_device(): lax.psum_scatter(partial_rows, 'tp', scatter_dimension=1, tiled=True)  89.9 us
    psum x1, blocking collectives, spread(): return lax.psum(kept, axis)  62.8 us
    ppermute x16, starting transfers between devices, shifted(): return lax.ppermute(x, axis, pairs)  44.6 us
    dot_general x1, matrix products, one_block(): jnp.einsum('kgql,lkd->qkgd', weight.astype(jnp.bfloat16), value_block, pr...  19.5 us
    dot_general x1, matrix products, one_block(): jnp.einsum('qkgd,lkd->kgql', query, key_block, preferred_element_type=jnp...  17.2 us
    unnamed x52, local copies, waits for them, and re-layouts  14.8 us
    concatenate x10, local copies, waits for them, and re-layouts, on_device(): keys_all = jnp.concatenate([piece[0] for piece in pieces] + [keys], axis=0)  12.6 us
    dot_general x1, matrix products, on_device(): partial_rows = jnp.dot(attended, w_out, preferred_element_type=jnp.float32)  8.81 us
  transfers between devices with their start and end apart: 17, of which 2 were waited for; matrix products, arithmetic and copies ran while one was open for 14% of the time, Pallas kernels for 0%

commit v1 on v0

--- a/solution.py
+++ b/solution.py
@@ -10,6 +10,12 @@
 SINKS = 4
 
 
+def add_all(array, axis):
+    pieces = lax.all_gather(array, axis, axis=0, tiled=False)
+    total = pieces.sum(axis=0)
+    return total
+
+
 def shifted(x, axis, by):
     devices = lax.axis_size(axis)
     pairs = [(i, i + by) for i in range(devices) if 0 <= i + by < devices]
@@ -18,7 +24,7 @@
 
 def spread(value, axis, source):
     kept = jnp.where(lax.axis_index(axis) == source, value, 0).astype(value.dtype)
-    return lax.psum(kept, axis)
+    return add_all(kept, axis)
 
 
 def rope_tables(positions):

time: 352 us -> 339 us (0.963)
  blocking collectives: 71.4 us -> 53.5 us
  starting transfers between devices: 44.7 us -> 58.5 us
  waiting for transfers between devices: 97.4 us -> 89.4 us
    psum x1 -> x0, blocking collectives: 62.8 us -> none  [spread(): return lax.psum(kept, axis)]
    all_gather x0 -> x2, blocking collectives: none -> 44.9 us  [add_all(): pieces = lax.all_gather(array, axis, axis=0, tiled=False)]
    ppermute x16, starting transfers between devices: 44.6 us -> 58.4 us  [shifted(): return lax.ppermute(x, axis, pairs)]
    ppermute x16, waiting for transfers between devices: 7.48 us -> 1.24 us  [shifted(): return lax.ppermute(x, axis, pairs)]
    unnamed x52 -> x48, local copies, waits for them, and re-layouts: 14.8 us -> 14.2 us
where the time goes in v1:
time: 339 us; the launch traced here: 337 us
  waiting for transfers between devices  89.4 us (26%)
  matrix products  59.2 us (17%)
  starting transfers between devices  58.5 us (17%)
  blocking collectives  53.5 us (16%)
  local copies, waits for them, and re-layouts  33.7 us (10%)
  other arithmetic  28.4 us (8%)
  between operations  14.5 us (4%)
    reduce_scatter x1, waiting for transfers between devices, on_device(): lax.psum_scatter(partial_rows, 'tp', scatter_dimension=1, tiled=True)  88.2 us
    ppermute x16, starting transfers between devices, shifted(): return lax.ppermute(x, axis, pairs)  58.4 us
    all_gather x2, blocking collectives, add_all(): pieces = lax.all_gather(array, axis, axis=0, tiled=False)  44.9 us
    dot_general x1, matrix products, one_block(): jnp.einsum('kgql,lkd->qkgd', weight.astype(jnp.bfloat16), value_block, pr...  19.4 us
    dot_general x1, matrix products, one_block(): jnp.einsum('qkgd,lkd->kgql', query, key_block, preferred_element_type=jnp...  17.2 us
    unnamed x48, local copies, waits for them, and re-layouts  14.2 us
    concatenate x10, local copies, waits for them, and re-layouts, on_device(): keys_all = jnp.concatenate([piece[0] for piece in pieces] + [keys], axis=0)  12.5 us
    dot_general x1, matrix products, on_device(): partial_rows = jnp.dot(attended, w_out, preferred_element_type=jnp.float32)  8.8 us
  transfers between devices with their start and end apart: 17, of which 2 were waited for; matrix products, arithmetic and copies ran while one was open for 14% of the time, Pallas kernels for 0%

profile of v1, /device:TPU:0, one launch (start us, length us, event | category | flops | bytes accessed | tf_op | source)
XLA Modules:
  0.0 337.2 jit_solution(17428150130586957969)
XLA Ops:
  8.7 3.5 %multiply_reduce_fusion = f32[512]{0:T(512)S(1)} fusion(bf16[512,4608]{1,0:T(8,128)(2,1)} %param.7), kind=kLoop, calls=%fused_computation.7 | loop fusion | flops 7077376 | bytes 4720640 | tf_op jit(solution)/shard_map/reduce_sum | solution.py:61
  15.5 4.4 %collective-permute-start.8 = (bf16[512,256]{0,1:T(8,128)(2,1)}, bf16[512,256]{0,1:T(8,128)(2,1)}, u32[]{:S(2)}, u32[]{:S(2)}) collective-permute-start(bf16[512,256]{0,1:T(8,128)(2,1)} %fusion.15), channel_id=1, source_target_pairs={{0,32},{4,36},{8,40},{12,44},{16,48},{20,52},{24,56},{28,60},{32,6... | collective-permute-start | bytes 786440 | tf_op jit(solution)/shard_map/ppermute | solution.py:22
  19.9 5.8 %collective-permute-start.9 = (bf16[512,256]{0,1:T(8,128)(2,1)}, bf16[512,256]{0,1:T(8,128)(2,1)}, u32[]{:S(2)}, u32[]{:S(2)}) collective-permute-start(bf16[512,256]{0,1:T(8,128)(2,1)} %fusion.15), channel_id=1, source_target_pairs={{0,28},{4,32},{8,36},{12,40},{16,44},{20,48},{24,52},{28,56},{32,6... | collective-permute-start | bytes 786440 | tf_op jit(solution)/shard_map/ppermute | solution.py:22
  25.7 3.3 collective-permute-start.10
  32.0 4.5 %convolution_convert_fusion = bf16[512,256]{1,0:T(8,128)(2,1)} fusion(bf16[4608,256]{1,0:T(8,128)(2,1)S(1)} %copy-done.14, f32[4608]{0:T(1024)S(1)} %copy-done.15, f32[512]{0:T(512)S(1)} %add_rsqrt_fusion.1, bf16[512,4608]{1,0:T(8,128)(2,1)} %param.7), kind=kOutput, calls=%fused_computation.16 | convolution fusion | flops 1217527808 | bytes 7360512 | tf_op jit(solution)/shard_map/dot_general | solution.py:49
  38.6 6.9 %fusion.29 = f32[512,512]{0,1:T(8,128)S(1)} fusion(bf16[4608,512]{1,0:T(8,128)(2,1)} %param.9, f32[4608]{0:T(1024)S(1)} %copy-done.15, f32[512]{0:T(512)S(1)} %add_rsqrt_fusion.1, bf16[512,4608]{1,0:T(8,128)(2,1)} %param.7), kind=kOutput, calls=%fused_computation.77 | convolution fusion | flops 2425356288 | bytes 10506240 | tf_op jit(solution)/shard_map/dot_general | solution.py:65
  52.1 4.7 %fusion.3 = pred[512,4608]{0,1:T(8,128)(4,1)} fusion(s32[4608]{0:T(1024)S(1)} %iota_add_fusion, s32[512]{0:T(512)S(1)} %get-tuple-element.42, pred[4608]{0:T(1024)(128)(4,1)S(1)} %broadcast_compare_fusion), kind=kLoop, calls=%fused_computation.9 | loop fusion | flops 11796480 | bytes 2384384 | tf_op jit(solution)/shard_map/while/body/eval_jaxpr/and | solution.py:103
  56.9 22.2 %all_gather.10 = bf16[32,4,256]{2,1,0:T(4,128)(2,1)S(1)} all-gather(bf16[1,4,256]{2,1,0:T(4,128)(2,1)S(1)} %copy.50), channel_id=1, replica_groups=mesh['ctx'=32,'tp'=4] {'ctx'}, dimensions={0}, use_global_device_ids=true | all-gather | bytes 67584 | tf_op jit(solution)/shard_map/all_gather | solution.py:14
  79.5 4.3 %collective-permute-start.1 = (bf16[512,256]{1,0:T(8,128)(2,1)}, bf16[512,256]{1,0:T(8,128)(2,1)S(1)}, u32[]{:S(2)}, u32[]{:S(2)}) collective-permute-start(bf16[512,256]{1,0:T(8,128)(2,1)} %convolution_convert_fusion), channel_id=1, source_target_pairs={{0,28},{4,32},{8,36},{12,40},{16,44},{20,48},{24,52},{28,56},{32,6... | collective-permute-start | bytes 786440 | tf_op jit(solution)/shard_map/ppermute | solution.py:22
  85.7 22.6 %all-gather.1 = bf16[32,4,256]{2,1,0:T(4,128)(2,1)S(1)} all-gather(bf16[1,4,256]{2,1,0:T(4,128)(2,1)S(1)} %fusion.22), channel_id=2, replica_groups=mesh['ctx'=32,'tp'=4] {'ctx'}, dimensions={0}, use_global_device_ids=true | all-gather | bytes 67584 | tf_op jit(solution)/shard_map/all_gather | solution.py:14
  109.5 4.0 %collective-permute-start.12 = (bf16[512,256]{0,1:T(8,128)(2,1)}, bf16[512,256]{0,1:T(8,128)(2,1)S(1)}, u32[]{:S(2)}, u32[]{:S(2)}) collective-permute-start(bf16[512,256]{0,1:T(8,128)(2,1)} %fusion.15), channel_id=1, source_target_pairs={{0,16},{4,20},{8,24},{12,28},{16,32},{20,36},{24,40},{28,44},{32,4... | collective-permute-start | bytes 786440 | tf_op jit(solution)/shard_map/ppermute | solution.py:22
  115.7 4.0 %collective-permute-start.2 = (bf16[512,256]{1,0:T(8,128)(2,1)}, bf16[512,256]{1,0:T(8,128)(2,1)S(1)}, u32[]{:S(2)}, u32[]{:S(2)}) collective-permute-start(bf16[512,256]{1,0:T(8,128)(2,1)} %convolution_convert_fusion), channel_id=1, source_target_pairs={{0,24},{4,28},{8,32},{12,36},{16,40},{20,44},{24,48},{28,52},{32,5... | collective-permute-start | bytes 786440 | tf_op jit(solution)/shard_map/ppermute | solution.py:22
  120.4 3.4 %collective-permute-start.3 = (bf16[512,256]{1,0:T(8,128)(2,1)}, bf16[512,256]{1,0:T(8,128)(2,1)S(1)}, u32[]{:S(2)}, u32[]{:S(2)}) collective-permute-start(bf16[512,256]{1,0:T(8,128)(2,1)} %convolution_convert_fusion), channel_id=1, source_target_pairs={{0,20},{4,24},{8,28},{12,32},{16,36},{20,40},{24,44},{28,48},{32,5... | collective-permute-start | bytes 786440 | tf_op jit(solution)/shard_map/ppermute | solution.py:22
  124.8 4.6 %collective-permute-start.4 = (bf16[512,256]{1,0:T(8,128)(2,1)}, bf16[512,256]{1,0:T(8,128)(2,1)S(1)}, u32[]{:S(2)}, u32[]{:S(2)}) collective-permute-start(bf16[512,256]{1,0:T(8,128)(2,1)} %convolution_convert_fusion), channel_id=1, source_target_pairs={{0,16},{4,20},{8,24},{12,28},{16,32},{20,36},{24,40},{28,44},{32,4... | collective-permute-start | bytes 786440 | tf_op jit(solution)/shard_map/ppermute | solution.py:22
  129.4 4.1 %collective-permute-start.14 = (bf16[512,256]{0,1:T(8,128)(2,1)}, bf16[512,256]{0,1:T(8,128)(2,1)}, u32[]{:S(2)}, u32[]{:S(2)}) collective-permute-start(bf16[512,256]{0,1:T(8,128)(2,1)} %fusion.15), channel_id=1, source_target_pairs={{0,8},{4,12},{8,16},{12,20},{16,24},{20,28},{24,32},{28,36},{32,40... | collective-permute-start | bytes 786440 | tf_op jit(solution)/shard_map/ppermute | solution.py:22
  138.7 5.1 %collective-permute-start.6 = (bf16[512,256]{1,0:T(8,128)(2,1)}, bf16[512,256]{1,0:T(8,128)(2,1)}, u32[]{:S(2)}, u32[]{:S(2)}) collective-permute-start(bf16[512,256]{1,0:T(8,128)(2,1)} %convolution_convert_fusion), channel_id=1, source_target_pairs={{0,8},{4,12},{8,16},{12,20},{16,24},{20,28},{24,32},{28,36},{32,40... | collective-permute-start | bytes 786440 | tf_op jit(solution)/shard_map/ppermute | solution.py:22
  143.8 4.3 %collective-permute-start.7 = (bf16[512,256]{1,0:T(8,128)(2,1)}, bf16[512,256]{1,0:T(8,128)(2,1)}, u32[]{:S(2)}, u32[]{:S(2)}) collective-permute-start(bf16[512,256]{1,0:T(8,128)(2,1)} %convolution_convert_fusion), channel_id=1, source_target_pairs={{0,4},{4,8},{8,12},{12,16},{16,20},{20,24},{24,28},{28,32},{32,36}... | collective-permute-start | bytes 786440 | tf_op jit(solution)/shard_map/ppermute | solution.py:22
  174.2 17.2 %fusion = (f32[2,2,512]{2,1,0:T(2,128)S(1)}, f32[2,4608,512,2]{2,1,3,0:T(8,128)}) fusion(pred[512,4608]{0,1:T(8,128)(4,1)S(1)} %copy-done.8, bf16[512,2,2,128]{3,0,2,1:T(8,128)(2,1)S(1)} %copy-done.10, bf16[4608,2,128]{2,0,1:T(8,128)(2,1)} %constant_dynamic-update-slice_fusion.9), kind=kOutput, calls=%fused_computation.2 | convolution fusion | flops 2453665792 | bytes 42999808 | tf_op jit(solution)/shard_map/while/body/eval_jaxpr/qkgd,lkd->kgql/dot_general | solution.py:91
  191.7 19.4 %fusion.7 = bf16[2,128,2,512]{3,1,2,0:T(8,128)(2,1)} fusion(f32[2,128,2,512]{3,1,2,0:T(8,128)S(1)} %fusion.20, bf16[4608,2,128,1]{0,2,3,1:T(8,128)(2,1)} %bitcast.86, f32[2,4608,512,2]{2,1,3,0:T(8,128)} %get-tuple-element.40, f32[2,2,512]{2,1,0:T(2,128)S(1)} %add.99, pred[512,4608]{0,1:T(8,128)(4,1)S(1)} %copy-done.8), kind=kOutput, calls=%fused_computation.15 | convolution fusion | flops 2463629312 | bytes 44048384 | tf_op jit(solution)/shard_map/while/body/eval_jaxpr/kgql,lkd->qkgd/dot_general | solution.py:111
  211.2 8.8 %fusion.32 = f32[512,4608]{1,0:T(8,128)} fusion(bf16[512,512]{0,1:T(8,128)(2,1)} %bitcast.87, bf16[512,4608]{1,0:T(8,128)(2,1)} %param.12), kind=kOutput, calls=%fused_computation.80 | convolution fusion | flops 2415919104 | bytes 14680064 | tf_op jit(solution)/shard_map/dot_general | solution.py:130
  220.0 7.2 %convert_element_type.60 = f32[512,4608]{1,0:T(8,128)} convert(bf16[512,4608]{1,0:T(8,128)(2,1)} %param.7) | non-fusion elementwise | flops 2359296 | bytes 14155776 | tf_op jit(solution)/shard_map/convert_element_type | solution.py:59
  227.2 88.2 %reduce-scatter.2.cloned.1.call-done = f32[512,1152]{1,0:T(8,128)} async-done(((f32[512,4608]{1,0:T(8,128)}), f32[512,1152]{1,0:T(8,128)}) %reduce-scatter.2.cloned.1.call-update) | async-done | bytes 2359312 | tf_op jit(solution)/shard_map/reduce_scatter | solution.py:131
  317.3 8.6 %all-reduce = (f32[512]{0:T(512)S(1)}, f32[512]{0:T(512)S(1)}) all-reduce(f32[512]{0:T(512)S(1)} %multiply_reduce_fusion.1, f32[512]{0:T(512)S(1)} %get-tuple-element.20), channel_id=1, replica_groups=mesh['ctx'=32,'tp'=4] {'tp'}, use_global_device_ids=true, to_apply=%region_7.8 | all-reduce | flops 1024 | bytes 8192 | tf_op jit(solution)/shard_map/psum | solution.py:133
  326.5 3.8 %add_convert_fusion = bf16[512,1152]{1,0:T(8,128)(2,1)} fusion(f32[512,1152]{1,0:T(8,128)} %reduce-scatter.2.cloned.1.call-done, f32[512,4608]{1,0:T(8,128)} %convert_element_type.60, s32[]{:T(128)S(6)} %select_n.37, f32[1152]{0:T(1024)S(1)} %copy-done.13, f32[512]{0:T(512)S(1)} %add_rsqrt_fusion), kind=kLoop, calls=%fused_computation.12 | loop fusion | flops 2359296 | bytes 5904900 | tf_op jit(solution)/shard_map/convert_element_type | solution.py:136
  (115 shorter events, 57.5 us)
Async XLA Ops:
  7.2 308.2 %reduce-scatter.2.cloned.1.call-start = ((), (), s32[]{:S(2)}) async-start(), calls=%async_computation.1 | async-start | bytes 11796480 | tf_op jit(solution)/shard_map/reduce_scatter | solution.py:131
  14.3 22.3 %copy-start.3 = (f32[512,256]{0,1:T(8,128)}, f32[512,256]{0,1:T(8,128)S(1)}, u32[]{:S(2)}) copy-start(f32[512,256]{0,1:T(8,128)S(1)} %fusion.30) | copy-start | bytes 1572868
  14.5 24.1 %copy-start.11 = (f32[512,128]{0,1:T(8,128)}, f32[512,128]{0,1:T(8,128)S(1)}, u32[]{:S(2)}) copy-start(f32[512,128]{0,1:T(8,128)S(1)} %copy.25) | copy-start | bytes 786436
  14.5 17.5 %copy-start.14 = (bf16[4608,256]{1,0:T(8,128)(2,1)S(1)}, bf16[4608,256]{1,0:T(8,128)(2,1)}, u32[]{:S(2)}) copy-start(bf16[4608,256]{1,0:T(8,128)(2,1)} %param.11) | copy-start | bytes 7077892
  14.6 22.0 %copy-start.4 = (f32[512,2,128]{0,2,1:T(8,128)}, f32[512,2,128]{0,2,1:T(8,128)S(1)}, u32[]{:S(2)}) copy-start(f32[512,2,128]{0,2,1:T(8,128)S(1)} %maximum_multiply_fusion.1) | copy-start | bytes 1572868
  15.5 64.0 %collective-permute-start.8 = (bf16[512,256]{0,1:T(8,128)(2,1)}, bf16[512,256]{0,1:T(8,128)(2,1)}, u32[]{:S(2)}, u32[]{:S(2)}) collective-permute-start(bf16[512,256]{0,1:T(8,128)(2,1)} %fusion.15), channel_id=1, source_target_pairs={{0,32},{4,36},{8,40},{12,44},{16,48},{20,52},{24,56},{28,60},{32,6... | collective-permute-start | bytes 786440 | tf_op jit(solution)/shard_map/ppermute | solution.py:22
  19.9 89.6 %collective-permute-start.9 = (bf16[512,256]{0,1:T(8,128)(2,1)}, bf16[512,256]{0,1:T(8,128)(2,1)}, u32[]{:S(2)}, u32[]{:S(2)}) collective-permute-start(bf16[512,256]{0,1:T(8,128)(2,1)} %fusion.15), channel_id=1, source_target_pairs={{0,28},{4,32},{8,36},{12,40},{16,44},{20,48},{24,52},{28,56},{32,6... | collective-permute-start | bytes 786440 | tf_op jit(solution)/shard_map/ppermute | solution.py:22
  25.7 87.9 %collective-permute-start.10 = (bf16[512,256]{0,1:T(8,128)(2,1)}, bf16[512,256]{0,1:T(8,128)(2,1)}, u32[]{:S(2)}, u32[]{:S(2)}) collective-permute-start(bf16[512,256]{0,1:T(8,128)(2,1)} %fusion.15), channel_id=1, source_target_pairs={{0,24},{4,28},{8,32},{12,36},{16,40},{20,44},{24,48},{28,52},{32,5... | collective-permute-start | bytes 786440 | tf_op jit(solution)/shard_map/ppermute | solution.py:22
  29.0 86.7 %collective-permute-start.11 = (bf16[512,256]{0,1:T(8,128)(2,1)}, bf16[512,256]{0,1:T(8,128)(2,1)}, u32[]{:S(2)}, u32[]{:S(2)}) collective-permute-start(bf16[512,256]{0,1:T(8,128)(2,1)} %fusion.15), channel_id=1, source_target_pairs={{0,20},{4,24},{8,28},{12,32},{16,36},{20,40},{24,44},{28,48},{32,5... | collective-permute-start | bytes 786440 | tf_op jit(solution)/shard_map/ppermute | solution.py:22
  36.6 83.8 %collective-permute-start = (bf16[512,256]{1,0:T(8,128)(2,1)}, bf16[512,256]{1,0:T(8,128)(2,1)}, u32[]{:S(2)}, u32[]{:S(2)}) collective-permute-start(bf16[512,256]{1,0:T(8,128)(2,1)} %convolution_convert_fusion), channel_id=1, source_target_pairs={{0,32},{4,36},{8,40},{12,44},{16,48},{20,52},{24,56},{28,60},{32,6... | collective-permute-start | bytes 786440 | tf_op jit(solution)/shard_map/ppermute | solution.py:22
  52.1 68.3 %copy-start.9 = (bf16[512,2,2,128]{3,0,2,1:T(8,128)(2,1)}, bf16[512,2,2,128]{3,0,2,1:T(8,128)(2,1)S(1)}, u32[]{:S(2)}) copy-start(bf16[512,2,2,128]{3,0,2,1:T(8,128)(2,1)S(1)} %fusion.14) | copy-start | bytes 1572868
  79.5 45.3 %collective-permute-start.1 = (bf16[512,256]{1,0:T(8,128)(2,1)}, bf16[512,256]{1,0:T(8,128)(2,1)S(1)}, u32[]{:S(2)}, u32[]{:S(2)}) collective-permute-start(bf16[512,256]{1,0:T(8,128)(2,1)} %convolution_convert_fusion), channel_id=1, source_target_pairs={{0,28},{4,32},{8,36},{12,40},{16,44},{20,48},{24,52},{28,56},{32,6... | collective-permute-start | bytes 786440 | tf_op jit(solution)/shard_map/ppermute | solution.py:22
  109.5 19.9 %collective-permute-start.12 = (bf16[512,256]{0,1:T(8,128)(2,1)}, bf16[512,256]{0,1:T(8,128)(2,1)S(1)}, u32[]{:S(2)}, u32[]{:S(2)}) collective-permute-start(bf16[512,256]{0,1:T(8,128)(2,1)} %fusion.15), channel_id=1, source_target_pairs={{0,16},{4,20},{8,24},{12,28},{16,32},{20,36},{24,40},{28,44},{32,4... | collective-permute-start | bytes 786440 | tf_op jit(solution)/shard_map/ppermute | solution.py:22
  113.6 19.9 %collective-permute-start.13 = (bf16[512,256]{0,1:T(8,128)(2,1)}, bf16[512,256]{0,1:T(8,128)(2,1)S(1)}, u32[]{:S(2)}, u32[]{:S(2)}) collective-permute-start(bf16[512,256]{0,1:T(8,128)(2,1)} %fusion.15), channel_id=1, source_target_pairs={{0,12},{4,16},{8,20},{12,24},{16,28},{20,32},{24,36},{28,40},{32,4... | collective-permute-start | bytes 786440 | tf_op jit(solution)/shard_map/ppermute | solution.py:22
  115.7 21.0 %collective-permute-start.2 = (bf16[512,256]{1,0:T(8,128)(2,1)}, bf16[512,256]{1,0:T(8,128)(2,1)S(1)}, u32[]{:S(2)}, u32[]{:S(2)}) collective-permute-start(bf16[512,256]{1,0:T(8,128)(2,1)} %convolution_convert_fusion), channel_id=1, source_target_pairs={{0,24},{4,28},{8,32},{12,36},{16,40},{20,44},{24,48},{28,52},{32,5... | collective-permute-start | bytes 786440 | tf_op jit(solution)/shard_map/ppermute | solution.py:22
  120.4 18.3 %collective-permute-start.3 = (bf16[512,256]{1,0:T(8,128)(2,1)}, bf16[512,256]{1,0:T(8,128)(2,1)S(1)}, u32[]{:S(2)}, u32[]{:S(2)}) collective-permute-start(bf16[512,256]{1,0:T(8,128)(2,1)} %convolution_convert_fusion), channel_id=1, source_target_pairs={{0,20},{4,24},{8,28},{12,32},{16,36},{20,40},{24,44},{28,48},{32,5... | collective-permute-start | bytes 786440 | tf_op jit(solution)/shard_map/ppermute | solution.py:22
  124.8 19.0 %collective-permute-start.4 = (bf16[512,256]{1,0:T(8,128)(2,1)}, bf16[512,256]{1,0:T(8,128)(2,1)S(1)}, u32[]{:S(2)}, u32[]{:S(2)}) collective-permute-start(bf16[512,256]{1,0:T(8,128)(2,1)} %convolution_convert_fusion), channel_id=1, source_target_pairs={{0,16},{4,20},{8,24},{12,28},{16,32},{20,36},{24,40},{28,44},{32,4... | collective-permute-start | bytes 786440 | tf_op jit(solution)/shard_map/ppermute | solution.py:22
  129.4 24.8 %collective-permute-start.14 = (bf16[512,256]{0,1:T(8,128)(2,1)}, bf16[512,256]{0,1:T(8,128)(2,1)}, u32[]{:S(2)}, u32[]{:S(2)}) collective-permute-start(bf16[512,256]{0,1:T(8,128)(2,1)} %fusion.15), channel_id=1, source_target_pairs={{0,8},{4,12},{8,16},{12,20},{16,24},{20,28},{24,32},{28,36},{32,40... | collective-permute-start | bytes 786440 | tf_op jit(solution)/shard_map/ppermute | solution.py:22
  133.5 14.7 %copy-start.12 = (bf16[512,256]{0,1:T(8,128)(2,1)}, bf16[512,256]{0,1:T(8,128)(2,1)S(1)}, u32[]{:S(2)}) copy-start(bf16[512,256]{0,1:T(8,128)(2,1)S(1)} %collective-permute-done.13) | copy-start | bytes 786436
  133.5 22.5 %collective-permute-start.15 = (bf16[512,256]{0,1:T(8,128)(2,1)}, bf16[512,256]{0,1:T(8,128)(2,1)}, u32[]{:S(2)}, u32[]{:S(2)}) collective-permute-start(bf16[512,256]{0,1:T(8,128)(2,1)} %fusion.15), channel_id=1, source_target_pairs={{0,4},{4,8},{8,12},{12,16},{16,20},{20,24},{24,28},{28,32},{32,36}... | collective-permute-start | bytes 786440 | tf_op jit(solution)/shard_map/ppermute | solution.py:22
  136.7 21.1 %collective-permute-start.5 = (bf16[512,256]{1,0:T(8,128)(2,1)}, bf16[512,256]{1,0:T(8,128)(2,1)}, u32[]{:S(2)}, u32[]{:S(2)}) collective-permute-start(bf16[512,256]{1,0:T(8,128)(2,1)} %convolution_convert_fusion), channel_id=1, source_target_pairs={{0,12},{4,16},{8,20},{12,24},{16,28},{20,32},{24,36},{28,40},{32,4... | collective-permute-start | bytes 786440 | tf_op jit(solution)/shard_map/ppermute | solution.py:22
  138.7 20.1 %collective-permute-start.6 = (bf16[512,256]{1,0:T(8,128)(2,1)}, bf16[512,256]{1,0:T(8,128)(2,1)}, u32[]{:S(2)}, u32[]{:S(2)}) collective-permute-start(bf16[512,256]{1,0:T(8,128)(2,1)} %convolution_convert_fusion), channel_id=1, source_target_pairs={{0,8},{4,12},{8,16},{12,20},{16,24},{20,28},{24,32},{28,36},{32,40... | collective-permute-start | bytes 786440 | tf_op jit(solution)/shard_map/ppermute | solution.py:22
  143.8 15.9 %collective-permute-start.7 = (bf16[512,256]{1,0:T(8,128)(2,1)}, bf16[512,256]{1,0:T(8,128)(2,1)}, u32[]{:S(2)}, u32[]{:S(2)}) collective-permute-start(bf16[512,256]{1,0:T(8,128)(2,1)} %convolution_convert_fusion), channel_id=1, source_target_pairs={{0,4},{4,8},{8,12},{12,16},{16,20},{20,24},{24,28},{28,32},{32,36}... | collective-permute-start | bytes 786440 | tf_op jit(solution)/shard_map/ppermute | solution.py:22
  227.2 99.3 %copy-start.13 = (f32[1152]{0:T(1024)S(1)}, f32[1152]{0:T(1024)}, u32[]{:S(2)}) copy-start(f32[1152]{0:T(1024)} %param.13) | copy-start | bytes 13828
  (10 other events, 53.1 us)
Sparse Core Ops, SparseCore 0:
  220.1 95.2 reduce-scatter.1
